TPU v7x, 512 devices: a whole 4x8x8 slice. The times are simulated.
512 devices in a mesh: rows: 32 (over y, x), vocab: 16 (over z, core).
Axes of the slice: x: 4, y: 8, z: 8, core: 2. Of those that a mesh axis runs over, the one named last changes fastest.
Arguments:
- hidden: bfloat16 [12288, 8192], P('rows', 'vocab'), may hold values from -128 to 128
- head: bfloat16 [8192, 8192], P('rows', 'vocab'), may hold values from -4 to 4
- targets: int32 [12288], P('rows'), may hold values from 0 to 128255
- live: int32 [12288], P('rows'), may hold values from 0 to 1, as said below
- prior_lse: float32 [12288], P('rows'), may hold values from 10 to 18
- prior_mean: float32 [12288], P('rows'), may hold values from 2 to 8
- prior_target: float32 [12288], P('rows'), may hold values from -12 to 12
- seq_lengths: int32 [32], replicated, may hold values from 1 to 768, 12288 in all
Outputs:
- logprob: float32 [12288], P(('rows', 'vocab'))
- entropy: float32 [12288], P(('rows', 'vocab'))
- seq_score: float32 [32], replicated
Inputs may be any that keep to these rules, and one draw needn't show every extreme that they name: Within the 384 rows of each index of rows, the live rows come first; every such index has at least 48 live rows and some index has all 384.
All inputs are finite; a program needn't handle non-finite values.
Results may differ from a plain program's by a relative error of at most 0.0003.
Values may be sent and summed in bfloat16 or wider, within the bound.
No kernel may reach another device: no remote copies, remote signals or barrier semaphores. Data moves between devices by JAX's collectives and lax.ppermute only.
A program may use at most 64 MiB of HBM per device.

v0:
```python
import jax
import jax.numpy as jnp
from jax import lax
from jax.sharding import PartitionSpec as P

VOCAB = 128256
SEQS = 32
GSIZE = 8


def finish_rows(block_peak, block_mass, block_moment, block_target, live, prior_lse, prior_mean):
    highest = jnp.maximum(block_peak, prior_lse)
    earlier = jnp.exp(prior_lse - highest)
    scaled = jnp.exp(block_peak - highest)
    total_mass = earlier + block_mass * scaled
    norm_log = highest + jnp.log(total_mass)
    average = (earlier * prior_mean + scaled * block_moment) / total_mass
    keeping = live.astype(jnp.float32)
    return (keeping * (block_target - norm_log), keeping * (norm_log - average))


def local(hidden, head, targets, live, prior_lse, prior_mean, prior_target, seq_lengths):
    rows_here = hidden.shape[0]
    cols_here = head.shape[1]
    spread = lax.axis_size("vocab")
    which = lax.axis_index("vocab")
    block_first = VOCAB - cols_here * spread
    first_col = block_first + which * cols_here
    gathered = lax.all_gather(hidden, "vocab", axis=1, tiled=True)
    logits = jnp.dot(
        gathered,
        lax.all_gather(head, "rows", axis=0, tiled=True),
        preferred_element_type=jnp.float32,
    )
    row_peak = jnp.max(logits, axis=1)
    weights = jnp.exp(logits - row_peak[:, None])
    row_mass = jnp.sum(weights, axis=1)
    moment = jnp.sum(weights * logits, axis=1)
    column = targets - first_col
    columns = lax.broadcasted_iota(jnp.int32, logits.shape, 1)
    picked = jnp.sum(jnp.where(columns == column[:, None], logits, jnp.zeros_like(logits)), axis=1)
    stats = jnp.stack([row_peak, row_mass, moment, picked])
    every = lax.all_gather(stats, "vocab", axis=0, tiled=False)
    peaks = every[:, 0]
    highest = jnp.max(peaks, axis=0)
    factor = jnp.exp(peaks - highest[None, :])
    mass_all = jnp.sum(every[:, 1] * factor, axis=0)
    moment_all = jnp.sum(every[:, 2] * factor, axis=0)
    picked_all = jnp.sum(every[:, 3], axis=0)
    block_target = jnp.where(targets >= block_first, picked_all, prior_target)
    logprob, entropy = finish_rows(
        highest, mass_all, moment_all, block_target, live, prior_lse, prior_mean
    )
    share = rows_here // spread
    begin = which * share
    logprob_share = lax.dynamic_slice_in_dim(logprob, begin, share, 0)
    entropy_share = lax.dynamic_slice_in_dim(entropy, begin, share, 0)
    global_rows = lax.axis_index("rows") * rows_here + jnp.arange(rows_here, dtype=jnp.int32)
    endings = jnp.cumsum(seq_lengths)
    member = jnp.sum((global_rows[:, None] >= endings[None, :]).astype(jnp.int32), axis=1)
    onehot = (member[:, None] == jnp.arange(SEQS, dtype=jnp.int32)[None, :]).astype(jnp.float32)
    partial_sums = jnp.sum(onehot * logprob[:, None], axis=0)
    sums = jnp.sum(lax.all_gather(partial_sums, "rows", axis=0, tiled=False), axis=0)
    seq_mean = sums / seq_lengths.astype(jnp.float32)
    grouped = seq_mean.reshape(SEQS // GSIZE, GSIZE)
    seq_score = (grouped - jnp.mean(grouped, axis=1, keepdims=True)).reshape(SEQS)
    return (logprob_share, entropy_share, seq_score)


def solution(mesh):
    return jax.shard_map(
        local,
        mesh=mesh,
        in_specs=(
            P("rows", "vocab"),
            P("rows", "vocab"),
            P("rows"),
            P("rows"),
            P("rows"),
            P("rows"),
            P("rows"),
            P(),
        ),
        out_specs=(P(("rows", "vocab")), P(("rows", "vocab")), P()),
        check_vma=False,
    )
```

profile of v0, /device:TPU:2, one launch (start us, length us, event | category | flops | bytes accessed | tf_op | source)
XLA Modules:
  0.0 275.6 jit_solution(6936003982868174059)
XLA Ops:
  7.2 0.0 all-gather.6.cloned.1.call-start
  7.2 0.7 all-gather.6.cloned.1.call-update
  7.9 0.0 all-gather.8.cloned.1.call-start
  7.9 0.7 all-gather.8.cloned.1.call-update
  8.7 0.7 copy.22
  9.4 0.1 reduce-window.8
  9.5 0.1 reduce.2
  9.6 1.3 dynamic-slice
  11.5 0.1 convert_reduce_fusion
  11.6 0.7 broadcast_subtract_fusion
  12.3 0.0 copy-start
  12.3 0.0 copy-start.1
  12.3 0.0 copy-start.2
  12.3 0.0 copy-start.3
  12.3 0.0 copy-start.4
  12.3 0.0 copy-start.5
  12.3 52.0 %all-gather.6.cloned.1.call-done = bf16[384,8192]{1,0:T(8,128)(2,1)} async-done(((bf16[384,512]{1,0:T(8,128)(2,1)}), bf16[384,8192]{1,0:T(8,128)(2,1)}) %all-gather.6.cloned.1.call-update) | async-done | bytes 6291472 | tf_op jit(solution)/shard_map/all_gather | solution.py:29
  64.3 103.5 %all-gather.8.cloned.1.call-done = bf16[8192,512]{1,0:T(8,128)(2,1)} async-done(((bf16[256,512]{1,0:T(8,128)(2,1)}), bf16[8192,512]{1,0:T(8,128)(2,1)}) %all-gather.8.cloned.1.call-update) | async-done | bytes 8388624 | tf_op jit(solution)/shard_map/all_gather | solution.py:32
  167.7 8.0 %fusion.7 = (f32[384]{0:T(512)S(1)}, f32[384,512]{1,0:T(8,128)S(1)}) fusion(bf16[384,8192]{1,0:T(8,128)(2,1)} %all-gather.6.cloned.1.call-done, bf16[8192,512]{1,0:T(8,128)(2,1)} %all-gather.8.cloned.1.call-done), kind=kOutput, calls=%fused_computation.30 | convolution fusion | flops 3221421568 | bytes 15468032 | tf_op jit(solution)/shard_map/dot_general | solution.py:30
  175.8 0.5 fusion
  176.3 18.3 %all-gather.2 = f32[16,4,384]{2,1,0:T(4,128)S(1)} all-gather(f32[1,4,384]{2,1,0:T(4,128)S(1)} %maximum_bitcast_fusion), channel_id=2, replica_groups=mesh['rows'=32,'vocab'=16] {'vocab'}, dimensions={0}, use_global_device_ids=true | all-gather | bytes 104448 | tf_op jit(solution)/shard_map/all_gather | solution.py:43
  194.6 0.1 fusion.6
  194.8 0.0 copy-done
  194.8 0.0 copy-done.1
  194.8 0.0 copy-done.2
  194.8 0.0 copy-done.3
  194.8 0.0 copy-done.4
  194.8 0.6 dynamic_slice.6
  195.4 0.6 dynamic_slice.7
  196.0 0.1 select_reduce_fusion.1
  196.1 0.2 dynamic-update-slice
  196.4 71.4 %all-reduce = f32[1024]{0:T(1024)S(1)} all-reduce(f32[1024]{0:T(1024)S(1)} %dynamic-update-slice), channel_id=3, replica_groups=mesh['rows'=32,'vocab'=16] {'rows'}, use_global_device_ids=true, to_apply=%add | all-reduce | flops 1024 | bytes 8192
  267.8 0.1 reshape.52
  267.9 0.0 copy-done.5
  267.9 0.1 reshape.50
  268.0 0.1 reduce_sum.99
  268.1 0.1 sub.55
  268.2 0.1 sub.56
  268.2 0.5 sub.57
  (12 shorter events, 0.1 us)
Async XLA Ops:
  7.2 57.1 %all-gather.6.cloned.1.call-start = ((), (), s32[]{:S(2)}) async-start(), calls=%async_computation | async-start | bytes 6684672 | tf_op jit(solution)/shard_map/all_gather | solution.py:29
  7.9 159.8 %all-gather.8.cloned.1.call-start = ((), (), s32[]{:S(2)}) async-start(), calls=%async_computation.1 | async-start | bytes 8650752 | tf_op jit(solution)/shard_map/all_gather | solution.py:32
  12.3 182.5 %copy-start = (s32[384]{0:T(512)S(1)}, s32[384]{0:T(512)}, u32[]{:S(2)}) copy-start(s32[384]{0:T(512)} %param.10) | copy-start | bytes 4612
  12.3 182.5 %copy-start.1 = (f32[384]{0:T(512)S(1)}, f32[384]{0:T(512)}, u32[]{:S(2)}) copy-start(f32[384]{0:T(512)} %param.13) | copy-start | bytes 4612
  12.3 182.5 %copy-start.2 = (s32[384]{0:T(512)S(1)}, s32[384]{0:T(512)}, u32[]{:S(2)}) copy-start(s32[384]{0:T(512)} %param.11) | copy-start | bytes 4612
  12.3 182.5 %copy-start.3 = (f32[384]{0:T(512)S(1)}, f32[384]{0:T(512)}, u32[]{:S(2)}) copy-start(f32[384]{0:T(512)} %param.12) | copy-start | bytes 4612
  12.3 182.5 %copy-start.4 = (f32[384]{0:T(512)S(1)}, f32[384]{0:T(512)}, u32[]{:S(2)}) copy-start(f32[384]{0:T(512)} %param.14) | copy-start | bytes 4612
  12.3 255.5 %copy-start.5 = (s32[32]{0:T(128)S(1)}, s32[32]{0:T(128)}, u32[]{:S(2)}) copy-start(s32[32]{0:T(128)} %param.15) | copy-start | bytes 388
Sparse Core Ops, SparseCore 0:
  10.1 54.0 all-gather.5
  67.4 100.2 all-gather.7
where the time goes:
time: 276 us
  waiting for transfers between devices  157 us (57%)
  blocking collectives  89.7 us (32%)
  between operations  14.8 us (5%)
  matrix products  8 us (3%)
  local copies, waits for them, and re-layouts  3.78 us (1%)
    all_gather x1, waiting for transfers between devices, local(): lax.all_gather(head, 'rows', axis=0, tiled=True)  103 us
    unnamed x1, blocking collectives  71.4 us
    all_gather x1, waiting for transfers between devices, local(): gathered = lax.all_gather(hidden, 'vocab', axis=1, tiled=True)  52 us
    all_gather x1, blocking collectives, local(): every = lax.all_gather(stats, 'vocab', axis=0, tiled=False)  18.3 us
    dot_general x1, matrix products, local(): jnp.dot(gathered, lax.all_gather(head, 'rows', axis=0, tiled=True), prefe...  8 us
  transfers between devices with their start and end apart: 2, of which 2 were waited for; matrix products, arithmetic and copies ran while one was open for 1% of the time, Pallas kernels for 0%

commit v1 on v0

--- a/solution.py
+++ b/solution.py
@@ -6,6 +6,12 @@
 VOCAB = 128256
 SEQS = 32
 GSIZE = 8
+
+
+def tiled_gather(x, axis, dim):
+    devices = lax.axis_size(axis)
+    repeats = [devices if d == dim else 1 for d in range(x.ndim)]
+    return lax.all_to_all(jnp.tile(x, repeats), axis, split_axis=dim, concat_axis=dim, tiled=True)
 
 
 def finish_rows(block_peak, block_mass, block_moment, block_target, live, prior_lse, prior_mean):
@@ -27,11 +33,7 @@
     block_first = VOCAB - cols_here * spread
     first_col = block_first + which * cols_here
     gathered = lax.all_gather(hidden, "vocab", axis=1, tiled=True)
-    logits = jnp.dot(
-        gathered,
-        lax.all_gather(head, "rows", axis=0, tiled=True),
-        preferred_element_type=jnp.float32,
-    )
+    logits = jnp.dot(gathered, tiled_gather(head, "rows", 0), preferred_element_type=jnp.float32)
     row_peak = jnp.max(logits, axis=1)
     weights = jnp.exp(logits - row_peak[:, None])
     row_mass = jnp.sum(weights, axis=1)

time: 276 us -> 333 us (1.21)
  the two profiles are of different devices: /device:TPU:2 before, /device:TPU:32 now
where the time goes in v1:
time: 333 us; the launch traced here: 332 us
  waiting for transfers between devices  183 us (55%)
  blocking collectives  106 us (32%)
  between operations  14.8 us (4%)
  starting transfers between devices  10.3 us (3%)
  local copies, waits for them, and re-layouts  8.22 us (2%)
  matrix products  8.04 us (2%)
    all_to_all x1, waiting for transfers between devices, tiled_gather(): lax.all_to_all(jnp.tile(x, repeats), axis, split_axis=dim, concat_axis=di...  129 us
    unnamed x1, blocking collectives  83.6 us
    all_gather x1, waiting for transfers between devices, local(): gathered = lax.all_gather(hidden, 'vocab', axis=1, tiled=True)  53.4 us
    all_gather x1, blocking collectives, local(): every = lax.all_gather(stats, 'vocab', axis=0, tiled=False)  22.7 us
    all_to_all x1, starting transfers between devices, tiled_gather(): lax.all_to_all(jnp.tile(x, repeats), axis, split_axis=dim, concat_axis=di...  10.3 us
    dot_general x1, matrix products, local(): jnp.dot(gathered, tiled_gather(head, 'rows', 0), preferred_element_type=j...  8.04 us
  transfers between devices with their start and end apart: 2, of which 2 were waited for; matrix products, arithmetic and copies ran while one was open for 0% of the time, Pallas kernels for 0%

profile of v1, /device:TPU:32, one launch (start us, length us, event | category | flops | bytes accessed | tf_op | source)
XLA Modules:
  0.0 332.4 jit_solution(10693106749679313728)
XLA Ops:
  7.2 5.1 %tile.2 = bf16[32,256,512]{2,1,0:T(8,128)(2,1)} broadcast(bf16[256,512]{1,0:T(8,128)(2,1)} %param.9), dimensions={1,2} | broadcast | bytes 8650752 | tf_op jit(solution)/shard_map/tile | solution.py:14
  12.3 0.0 copy-start.5
  12.3 0.0 copy-start
  12.3 10.3 %all-to-all-start = ((bf16[32,256,512]{2,1,0:T(8,128)(2,1)}), bf16[32,256,512]{2,1,0:T(8,128)(2,1)}, u32[]{:S(2)}, u32[]{:S(2)}) async-start(bf16[32,256,512]{2,1,0:T(8,128)(2,1)} %tile.2), calls=%async_computation | async-start | bytes 16777216 | tf_op jit(solution)/shard_map/all_to_all | solution.py:14
  22.5 0.0 all-gather.5.cloned.1.call-start
  22.6 0.7 all-gather.5.cloned.1.call-update
  23.3 0.0 copy-done.5
  23.3 0.1 copy.22
  23.4 0.1 reduce-window.8
  23.4 0.1 reduce.2
  23.6 1.3 dynamic-slice
  25.5 0.1 convert_reduce_fusion
  25.6 0.0 copy-done
  25.6 53.4 %all-gather.5.cloned.1.call-done = bf16[384,8192]{1,0:T(8,128)(2,1)} async-done(((bf16[384,512]{1,0:T(8,128)(2,1)}), bf16[384,8192]{1,0:T(8,128)(2,1)}) %all-gather.5.cloned.1.call-update) | async-done | bytes 6291472 | tf_op jit(solution)/shard_map/all_gather | solution.py:35
  79.0 128.8 %all-to-all-done = bf16[32,256,512]{2,1,0:T(8,128)(2,1)} async-done(((bf16[32,256,512]{2,1,0:T(8,128)(2,1)}), bf16[32,256,512]{2,1,0:T(8,128)(2,1)}, u32[]{:S(2)}, u32[]{:S(2)}) %all-to-all-start) | async-done | bytes 8388640 | tf_op jit(solution)/shard_map/all_to_all | solution.py:14
  207.9 0.0 copy-start.1
  207.9 0.0 copy-start.2
  207.9 0.0 copy-start.3
  207.9 0.0 copy-start.4
  207.9 8.0 %fusion.7 = (f32[384]{0:T(512)S(1)}, f32[384,512]{1,0:T(8,128)S(1)}) fusion(bf16[384,8192]{1,0:T(8,128)(2,1)} %all-gather.5.cloned.1.call-done, bf16[8192,512]{1,0:T(8,128)(2,1)} %bitcast), kind=kOutput, calls=%fused_computation.30 | convolution fusion | flops 3221421568 | bytes 15468032 | tf_op jit(solution)/shard_map/dot_general | solution.py:36
  215.9 0.5 fusion
  216.5 22.7 %all-gather.2 = f32[16,4,384]{2,1,0:T(4,128)S(1)} all-gather(f32[1,4,384]{2,1,0:T(4,128)S(1)} %maximum_bitcast_fusion), channel_id=2, replica_groups=mesh['rows'=32,'vocab'=16] {'vocab'}, dimensions={0}, use_global_device_ids=true | all-gather | bytes 104448 | tf_op jit(solution)/shard_map/all_gather | solution.py:45
  239.2 0.1 fusion.6
  239.3 0.0 copy-done.1
  239.4 0.0 copy-done.2
  239.4 0.0 copy-done.3
  239.4 0.0 copy-done.4
  239.4 0.1 select_reduce_fusion.1
  239.5 0.2 dynamic-update-slice
  239.8 83.6 %all-reduce = f32[1024]{0:T(1024)S(1)} all-reduce(f32[1024]{0:T(1024)S(1)} %dynamic-update-slice), channel_id=3, replica_groups=mesh['rows'=32,'vocab'=16] {'rows'}, use_global_device_ids=true, to_apply=%add | all-reduce | flops 1024 | bytes 8192
  323.4 0.1 reshape.59
  323.5 0.1 reshape.57
  323.6 0.1 reduce_sum.99
  323.7 0.1 sub.55
  323.8 0.1 sub.56
  323.8 0.5 sub.57
  324.4 0.6 dynamic_slice.6
  325.0 0.6 dynamic_slice.7
  (13 shorter events, 0.1 us)
Async XLA Ops:
  12.3 11.0 %copy-start.5 = (s32[32]{0:T(128)S(1)}, s32[32]{0:T(128)}, u32[]{:S(2)}) copy-start(s32[32]{0:T(128)} %param.15) | copy-start | bytes 388
  12.3 13.3 %copy-start = (s32[384]{0:T(512)S(1)}, s32[384]{0:T(512)}, u32[]{:S(2)}) copy-start(s32[384]{0:T(512)} %param.10) | copy-start | bytes 4612
  12.3 195.6 %all-to-all-start = ((bf16[32,256,512]{2,1,0:T(8,128)(2,1)}), bf16[32,256,512]{2,1,0:T(8,128)(2,1)}, u32[]{:S(2)}, u32[]{:S(2)}) async-start(bf16[32,256,512]{2,1,0:T(8,128)(2,1)} %tile.2), calls=%async_computation | async-start | bytes 16777216 | tf_op jit(solution)/shard_map/all_to_all | solution.py:14
  22.5 56.5 %all-gather.5.cloned.1.call-start = ((), (), s32[]{:S(2)}) async-start(), calls=%async_computation.1 | async-start | bytes 6684672 | tf_op jit(solution)/shard_map/all_gather | solution.py:35
  207.9 31.5 %copy-start.1 = (f32[384]{0:T(512)S(1)}, f32[384]{0:T(512)}, u32[]{:S(2)}) copy-start(f32[384]{0:T(512)} %param.13) | copy-start | bytes 4612
  207.9 31.5 %copy-start.2 = (s32[384]{0:T(512)S(1)}, s32[384]{0:T(512)}, u32[]{:S(2)}) copy-start(s32[384]{0:T(512)} %param.11) | copy-start | bytes 4612
  207.9 31.5 %copy-start.3 = (f32[384]{0:T(512)S(1)}, f32[384]{0:T(512)}, u32[]{:S(2)}) copy-start(f32[384]{0:T(512)} %param.12) | copy-start | bytes 4612
  207.9 31.5 %copy-start.4 = (f32[384]{0:T(512)S(1)}, f32[384]{0:T(512)}, u32[]{:S(2)}) copy-start(f32[384]{0:T(512)} %param.14) | copy-start | bytes 4612
Sparse Core Ops, SparseCore 0:
  25.5 53.4 all-gather.4
